TPU v7x, 256 devices: a whole 4x4x8 slice. The times are simulated.
256 devices in a mesh: dp: 8 (over x, z_hi), tensor: 32 (over y, z_lo, core).
Axes of the slice: x: 4, y: 4, z: 8 (z_hi: 2, z_lo: 4; z = z_hi * 4 + z_lo), core: 2. Of those that a mesh axis runs over, the one named last changes fastest.
Arguments:
- tokens: bfloat16 [8, 4096, 1280], P('dp', 'tensor'), may hold values from -6 to 6
- segment_ids: int32 [8, 4096], P('dp', 'tensor'), may hold values from 0 to 3, never falling along the last dimension, each value on 1 to 2048 neighbouring positions
- pack_of_group: int32 [32], replicated, may hold values from 0 to 31, each once
- w_qkv: bfloat16 [1280, 1920], replicated, may hold values from -0.11320094 to 0.11320094
- qk_gain: float32 [640], replicated, may hold values from 0.5 to 7
- w_out: bfloat16 [640, 1280], replicated, may hold values from -0.25 to 0.25
- alpha_attn: float32 [1280], replicated, may hold values from 0.05 to 0.6
- w_up: bfloat16 [1280, 5120], P(None, 'dp'), may hold values from -0.15625 to 0.15625
- w_gate: bfloat16 [1280, 5120], P(None, 'dp'), may hold values from -0.15625 to 0.15625
- up_gain: float32 [5120], P('dp'), may hold values from 0.5 to 2
- gate_gain: float32 [5120], P('dp'), may hold values from 0.5 to 2
- w_down: bfloat16 [5120, 1280], P('dp'), may hold values from -0.078125 to 0.078125
- alpha_mlp: float32 [1280], replicated, may hold values from 0.05 to 0.6
- w_vocab: bfloat16 [1280, 32000], P(None, ('dp', 'tensor')), may hold values from -0.15625 to 0.15625
- logit_gain: bfloat16 [32000], P(('dp', 'tensor')), may hold values from 1 to 10
Outputs:
- result_rows: bfloat16 [8, 4096, 1280], P('dp', 'tensor')
- request_norm: float32 [32], replicated
- max_logit: float32 [32], replicated
Inputs may be any that keep to these rules, and one draw needn't show every extreme that they name: `segment_ids`: within a pack the request numbers never fall, every request 0 to 3 has one or more tokens, and one request has exactly 2048 tokens.
All inputs are finite; a program needn't handle non-finite values.
Results may differ from a plain program's by a relative error of at most 0.013.
Values may be sent and summed in bfloat16 or wider, within the bound.
No kernel may reach another device: no remote copies, remote signals or barrier semaphores. Data moves between devices by JAX's collectives and lax.ppermute only.
A program may use at most 128 MiB of HBM per device.

v0:
```python
import math
import jax
import jax.numpy as jnp
from jax import lax
from jax.sharding import PartitionSpec as P

HEADS = 10
HD = 64
REQS = 4
EPSILON = 1e-06
NEGATIVE = -1e30


def normalize(values):
    return values * lax.rsqrt(jnp.mean(values * values, axis=-1, keepdims=True) + EPSILON)


def head_norm(values, qk_gain):
    reshaped = values.reshape(values.shape[0], HEADS, HD)
    return (normalize(reshaped) * qk_gain.reshape(HEADS, HD)).astype(jnp.bfloat16)


def local(
    tokens,
    segment_ids,
    pack_of_group,
    w_qkv,
    qk_gain,
    w_out,
    alpha_attn,
    w_up,
    w_gate,
    up_gain,
    gate_gain,
    w_down,
    alpha_mlp,
    w_vocab,
    logit_gain,
):
    row_count = tokens.shape[1]
    head_width = HEADS * HD
    segments = segment_ids[0]
    tensor_index = lax.axis_index("tensor")
    positions = tensor_index * row_count + jnp.arange(row_count, dtype=jnp.int32)
    request_numbers = jnp.arange(REQS, dtype=jnp.int32)
    start_rows = normalize(tokens[0].astype(jnp.float32)).astype(jnp.bfloat16)
    projected = jnp.dot(start_rows, w_qkv, preferred_element_type=jnp.float32)
    queries = head_norm(projected[:, :head_width], qk_gain)
    key_rows = head_norm(projected[:, head_width : 2 * head_width], qk_gain).reshape(
        row_count, head_width
    )
    value_rows = projected[:, 2 * head_width :].astype(jnp.bfloat16)
    score_scale = 1.0 / math.sqrt(HD)
    offset = jnp.int32(0)
    state_now = (
        jnp.full((HEADS, row_count), NEGATIVE, jnp.float32),
        jnp.zeros((HEADS, row_count), jnp.float32),
        jnp.zeros((HEADS, row_count, HD), jnp.float32),
    )
    key_all = lax.all_gather(key_rows, "tensor", axis=0, tiled=True)
    value_all = lax.all_gather(value_rows, "tensor", axis=0, tiled=True)
    seg_all = lax.all_gather(segments, "tensor", axis=0, tiled=True)
    tally = jnp.sum((seg_all[:, None] == request_numbers[None, :]).astype(jnp.int32), axis=0)
    total_keys = key_all.shape[0]
    step_size = math.gcd(total_keys, 512)
    for begin in range(0, total_keys, step_size):
        key_part = key_all[begin : begin + step_size]
        value_part = value_all[begin : begin + step_size]
        seg_part = seg_all[begin : begin + step_size]
        key_pos = offset + begin + jnp.arange(step_size, dtype=jnp.int32)
        update_running_max, update_weight_sum, update_weighted = state_now
        key_count = key_part.shape[0]
        key_heads = key_part.reshape(key_count, HEADS, HD)
        value_heads = value_part.reshape(key_count, HEADS, HD)
        scores = (
            jnp.einsum("qhd,khd->hqk", queries, key_heads, preferred_element_type=jnp.float32)
            * score_scale
        )
        allowed = (seg_part[None, :] == segments[:, None]) & (
            key_pos[None, :] <= positions[:, None]
        )
        new_max = jnp.maximum(
            update_running_max, jnp.max(jnp.where(allowed[None], scores, NEGATIVE), axis=2)
        )
        weights = jnp.where(allowed[None], jnp.exp(scores - new_max[:, :, None]), 0.0)
        factor = jnp.exp(update_running_max - new_max)
        update_weight_sum = update_weight_sum * factor + jnp.sum(weights, axis=2)
        update_weighted = update_weighted * factor[:, :, None] + jnp.einsum(
            "hqk,khd->hqd",
            weights.astype(jnp.bfloat16),
            value_heads,
            preferred_element_type=jnp.float32,
        )
        state_now = (new_max, update_weight_sum, update_weighted)
    folded, tally = (state_now, tally)
    running_max, weight_sum, weighted = folded
    attended = (
        (weighted / weight_sum[:, :, None])
        .transpose(1, 0, 2)
        .reshape(row_count, head_width)
        .astype(jnp.bfloat16)
    )
    attn_rows = normalize(jnp.dot(attended, w_out, preferred_element_type=jnp.float32))
    residual_in = start_rows.astype(jnp.float32)
    mid_rows = normalize(residual_in + alpha_attn * (attn_rows - residual_in)).astype(jnp.bfloat16)
    received = lax.all_gather(mid_rows, "dp", axis=0, tiled=True)
    up_proj = jnp.dot(received, w_up, preferred_element_type=jnp.float32) * up_gain
    gate_proj = jnp.dot(received, w_gate, preferred_element_type=jnp.float32) * gate_gain
    hidden = (up_proj * jax.nn.silu(gate_proj)).astype(jnp.bfloat16)
    mixed_sum = lax.psum_scatter(
        jnp.dot(hidden, w_down, preferred_element_type=jnp.float32).astype(jnp.bfloat16),
        "dp",
        scatter_dimension=0,
        tiled=True,
    ).astype(jnp.float32)
    mlp_rows = normalize(mixed_sum)
    residual_mid = mid_rows.astype(jnp.float32)
    result_rows = normalize(residual_mid + alpha_mlp * (mlp_rows - residual_mid)).astype(
        jnp.bfloat16
    )
    request_ends = jnp.cumsum(tally) - 1
    same_request = segments[:, None] == request_numbers[None, :]
    row_end = jnp.sum(jnp.where(same_request, request_ends[None, :], 0), axis=1)
    is_last = positions == row_end
    member = same_request.astype(jnp.float32)
    chosen = member * is_last[:, None].astype(jnp.float32)
    result_f32 = result_rows.astype(jnp.float32)
    row_sums = jnp.dot(member.T, result_f32, precision=lax.Precision.HIGHEST)
    last_rows = jnp.dot(chosen.T, result_f32, precision=lax.Precision.HIGHEST)
    counts = jnp.sum(member, axis=0)
    row_sums, last_rows, counts = (
        lax.psum(row_sums.astype(jnp.bfloat16), "tensor").astype(jnp.float32),
        lax.psum(last_rows.astype(jnp.bfloat16), "tensor").astype(jnp.float32),
        lax.psum(counts.astype(jnp.bfloat16), "tensor").astype(jnp.float32),
    )
    request_mean = row_sums / counts[:, None]
    group_norm = jnp.sqrt(jnp.mean(request_mean * request_mean, axis=1))
    slot_count = lax.axis_size("dp") * REQS
    every_last, every_norm = (
        lax.all_gather(last_rows, "dp", axis=0, tiled=True),
        lax.all_gather(group_norm, "dp", axis=0, tiled=True),
    )
    logits = jnp.dot(
        every_last.astype(jnp.bfloat16), w_vocab, preferred_element_type=jnp.float32
    ) * logit_gain.astype(jnp.float32)
    every_max = lax.pmax(jnp.max(logits, axis=1), ("dp", "tensor"))
    placement = (pack_of_group[:, None] == jnp.arange(slot_count, dtype=jnp.int32)[None, :]).astype(
        jnp.float32
    )
    request_norm = jnp.dot(every_norm, placement, precision=lax.Precision.HIGHEST)
    max_logit = jnp.dot(every_max, placement, precision=lax.Precision.HIGHEST)
    return (result_rows[None], request_norm, max_logit)


def solution(mesh):
    return jax.shard_map(
        local,
        mesh=mesh,
        in_specs=(
            P("dp", "tensor", None),
            P("dp", "tensor"),
            P(),
            P(),
            P(),
            P(),
            P(),
            P(None, "dp"),
            P(None, "dp"),
            P("dp"),
            P("dp"),
            P("dp", None),
            P(),
            P(None, ("dp", "tensor")),
            P(("dp", "tensor")),
        ),
        out_specs=(P("dp", "tensor", None), P(), P()),
        check_vma=False,
    )
```

profile of v0, /device:TPU:1, one launch (start us, length us, event | category | flops | bytes accessed | tf_op | source)
XLA Modules:
  0.0 689.7 jit_solution(16697699601182889394)
XLA Ops:
  7.2 1.2 fusion.143
  8.5 3.4 fusion.186
  14.2 46.0 %all-gather = s32[1,4096]{1,0:T(1,128)S(1)} all-gather(s32[1,128]{1,0:T(1,128)S(1)} %copy-done.26), channel_id=2, replica_groups=mesh['dp'=8,'tensor'=32] {'tensor'}, dimensions={1}, use_global_device_ids=true | all-gather | bytes 16896 | tf_op jit(solution)/shard_map/all_gather | solution.py:62
  60.5 1.2 fusion.145
  61.7 19.2 %all-gather.8.cloned.1.call-done = bf16[4096,640]{1,0:T(8,128)(2,1)} async-done(((bf16[128,640]{1,0:T(8,128)(2,1)}), bf16[4096,640]{1,0:T(8,128)(2,1)}) %all-gather.8.cloned.1.call-update) | async-done | bytes 5242896 | tf_op jit(solution)/shard_map/all_gather | solution.py:61
  80.8 4.5 fusion.191
  85.3 2.2 copy.88
  87.5 58.2 %all-gather.6.cloned.1.call-done = bf16[4096,640]{1,0:T(8,128)(2,1)} async-done(((bf16[128,640]{1,0:T(8,128)(2,1)}), bf16[4096,640]{1,0:T(8,128)(2,1)}) %all-gather.6.cloned.1.call-update) | async-done | bytes 5242896 | tf_op jit(solution)/shard_map/all_gather | solution.py:60
  145.7 4.9 fusion.192
  150.6 2.2 copy.77
  152.8 2.2 copy.91
  154.9 2.2 copy.89
  157.1 2.2 copy.87
  159.3 2.2 copy.85
  161.5 2.2 copy.83
  163.7 2.2 copy.81
  165.9 2.2 copy.79
  168.1 2.2 copy.92
  170.3 2.2 copy.90
  172.4 2.2 copy.86
  174.6 2.2 copy.84
  176.8 2.2 copy.82
  179.0 1.1 copy.80
  180.1 1.1 copy.78
  181.2 1.8 select_reduce_fusion.6
  190.2 1.8 fusion.4
  192.0 0.7 fusion.100
  193.1 0.7 fusion.124
  193.9 1.6 fusion.12
  195.5 0.7 fusion.127
  196.6 0.7 fusion.94
  197.3 1.6 fusion
  199.0 0.7 fusion.103
  199.7 1.6 fusion.8
  201.4 0.8 fusion.130
  202.5 0.8 fusion.137
  204.8 1.0 multiply_convert_fusion.2
  206.1 81.0 %all-gather.10.cloned.1.call-done = bf16[1024,1280]{1,0:T(8,128)(2,1)} async-done(((bf16[128,1280]{1,0:T(8,128)(2,1)}), bf16[1024,1280]{1,0:T(8,128)(2,1)}) %all-gather.10.cloned.1.call-update) | async-done | bytes 2621456 | tf_op jit(solution)/shard_map/all_gather | solution.py:106
  287.2 5.9 fusion.194
  293.1 8.4 %convolution_convert_fusion = bf16[1024,1280]{1,0:T(8,128)(2,1)} fusion(bf16[640,1280]{1,0:T(8,128)(2,1)S(1)} %copy-done, f32[1024,640]{1,0:T(8,128)} %fusion.194, bf16[1024,1280]{1,0:T(8,128)(2,1)} %all-gather.10.cloned.1.call-done, bf16[1280,640]{1,0:T(8,128)(2,1)S(1)} %copy-done.27, f32[640]{0:T(1024)S(1)} %copy-done.28, f32[640]{0:T(1024)S(1)} %copy-done.29), kind=kOutput, calls=%fused_computation | convolution fusion | flops 3361996800 | bytes 11146240 | tf_op jit(solution)/shard_map/dot_general | solution.py:111
  304.0 94.9 %reduce-scatter.2.cloned.1.call-done = bf16[128,1280]{1,0:T(8,128)(2,1)} async-done(((bf16[1024,1280]{1,0:T(8,128)(2,1)}), bf16[128,1280]{1,0:T(8,128)(2,1)}) %reduce-scatter.2.cloned.1.call-update) | async-done | bytes 327696 | tf_op jit(solution)/shard_map/reduce_scatter | solution.py:110
  398.9 1.1 fusion.142
  400.1 1.3 multiply_reduce_fusion
  401.4 1.4 multiply_convert_fusion.1
  403.2 130.5 %all-reduce.1 = (bf16[4,1280]{1,0:T(4,128)(2,1)S(1)}, bf16[4]{0:T(256)(128)(2,1)S(1)}, bf16[4,1280]{1,0:T(4,128)(2,1)S(1)}) all-reduce(bf16[4,1280]{1,0:T(4,128)(2,1)S(1)} %convolution_convert_fusion.2, bf16[4]{0:T(256)(128)(2,1)S(1)} %convert_reduce_fusion.1, ...), channel_id=1, replica_groups=mesh['dp'=8,'tensor'=32] {'tensor'}, use_global_device_ids=true, to_apply=%region_24.25 | all-reduce | flops 10244 | bytes 40976 | tf_op jit(solution)/shard_map/psum | solution.py:132
  533.7 37.8 %all-gather.1 = bf16[8,4,1280]{2,1,0:T(4,128)(2,1)S(1)} all-gather(bf16[1,4,1280]{2,1,0:T(4,128)(2,1)S(1)} %bitcast.282), channel_id=1, replica_groups=mesh['dp'=8,'tensor'=32] {'dp'}, dimensions={0}, use_global_device_ids=true | all-gather | bytes 92160 | tf_op jit(solution)/shard_map/all_gather | solution.py:140
  572.1 23.2 %all-reduce = f32[32]{0:T(128)S(1)} all-reduce(f32[32]{0:T(128)S(1)} %sqrt_dynamic-update-slice_fusion), channel_id=1, replica_groups=mesh['dp'=8,'tensor'=32] {'dp'}, use_global_device_ids=true, to_apply=%add | all-reduce | flops 32 | bytes 256
  595.3 86.5 %pmax.7 = f32[32]{0:T(128)S(1)} all-reduce(f32[32]{0:T(128)S(1)} %fusion.133), channel_id=1, replica_groups=mesh['dp'=8,'tensor'=32] {'dp','tensor'}, use_global_device_ids=true, to_apply=%region_33.34 | all-reduce | flops 32 | bytes 256 | tf_op jit(solution)/shard_map/pmax | solution.py:146
  (132 shorter events, 16.5 us)
Async XLA Ops:
  7.2 285.9 %copy-start = (bf16[640,1280]{1,0:T(8,128)(2,1)S(1)}, bf16[640,1280]{1,0:T(8,128)(2,1)}, u32[]{:S(2)}) copy-start(bf16[640,1280]{1,0:T(8,128)(2,1)} %param.26) | copy-start | bytes 4915204
  7.2 73.7 %all-gather.8.cloned.1.call-start = ((), (), s32[]{:S(2)}) async-start(), calls=%async_computation.2 | async-start | bytes 5406720 | tf_op jit(solution)/shard_map/all_gather | solution.py:61
  11.9 1.2 copy-start.25
  12.6 1.6 copy-start.26
  12.6 133.1 %all-gather.6.cloned.1.call-start = ((), (), s32[]{:S(2)}) async-start(), calls=%async_computation.1 | async-start | bytes 5406720 | tf_op jit(solution)/shard_map/all_gather | solution.py:60
  13.9 273.3 %all-gather.10.cloned.1.call-start = ((), (), s32[]{:S(2)}) async-start(), calls=%async_computation.3 | async-start | bytes 2949120 | tf_op jit(solution)/shard_map/all_gather | solution.py:106
  180.1 2.9 copy-start.10
  181.2 1.8 copy-start.21
  183.0 1.1 copy-start.9
  183.0 1.1 copy-start.20
  183.7 1.1 copy-start.8
  184.7 1.1 copy-start.7
  185.5 1.1 copy-start.6
  186.5 1.1 copy-start.5
  187.3 1.1 copy-start.4
  188.3 1.1 copy-start.19
  190.2 1.8 copy-start.18
  192.0 1.1 copy-start.17
  193.8 1.6 copy-start.15
  195.5 1.1 copy-start.16
  197.3 1.6 copy-start.14
  199.7 1.7 copy-start.13
  201.4 1.1 copy-start.12
  202.5 1.4 copy-start.11
  202.5 2.0 copy-start.23
  203.3 1.2 copy-start.1
  205.8 87.3 %copy-start.27 = (bf16[1280,640]{1,0:T(8,128)(2,1)S(1)}, bf16[1280,640]{1,0:T(8,128)(2,1)}, u32[]{:S(2)}) copy-start(bf16[1280,640]{1,0:T(8,128)(2,1)} %param.23) | copy-start | bytes 4915204
  205.8 87.2 %copy-start.28 = (f32[640]{0:T(1024)S(1)}, f32[640]{0:T(1024)}, u32[]{:S(2)}) copy-start(f32[640]{0:T(1024)} %param.25) | copy-start | bytes 7684
  205.8 87.2 %copy-start.29 = (f32[640]{0:T(1024)S(1)}, f32[640]{0:T(1024)}, u32[]{:S(2)}) copy-start(f32[640]{0:T(1024)} %param.24) | copy-start | bytes 7684
  205.9 193.1 %reduce-scatter.2.cloned.1.call-start = ((), (), s32[]{:S(2)}) async-start(), calls=%async_computation.4 | async-start | bytes 2949120 | tf_op jit(solution)/shard_map/reduce_scatter | solution.py:110
  301.5 0.7 copy-start.30
  301.5 0.7 copy-start.32
  301.5 98.5 %copy-start.2 = (bf16[128,1280]{1,0:T(8,128)(2,1)S(1)}, bf16[128,1280]{1,0:T(8,128)(2,1)}, u32[]{:S(2)}) copy-start(bf16[128,1280]{1,0:T(8,128)(2,1)} %multiply_convert_fusion.2) | copy-start | bytes 983044
  301.5 98.5 %copy-start.24 = (f32[1280]{0:T(1024)S(1)}, f32[1280]{0:T(1024)}, u32[]{:S(2)}) copy-start(f32[1280]{0:T(1024)} %param.27) | copy-start | bytes 15364
  301.5 270.3 %copy-start.22 = (bf16[1280,125]{1,0:T(8,128)(2,1)S(1)}, bf16[1280,125]{1,0:T(8,128)(2,1)}, u32[]{:S(2)}) copy-start(bf16[1280,125]{1,0:T(8,128)(2,1)} %param.28) | copy-start | bytes 960004
  301.5 380.2 %copy-start.31 = (s32[32]{0:T(128)S(1)}, s32[32]{0:T(128)}, u32[]{:S(2)}) copy-start(s32[32]{0:T(128)} %param.17) | copy-start | bytes 388
  402.8 280.4 %copy-start.3 = (bf16[128,1280]{1,0:T(8,128)(2,1)}, bf16[128,1280]{1,0:T(8,128)(2,1)S(1)}, u32[]{:S(2)}) copy-start(bf16[128,1280]{1,0:T(8,128)(2,1)S(1)} %multiply_convert_fusion.1) | copy-start | bytes 983044
Sparse Core Ops, SparseCore 0:
  12.7 68.0 all-gather.7
  82.7 62.9 all-gather.5
  205.9 81.1 all-gather.9
  301.7 97.1 reduce-scatter.1
where the time goes:
time: 691 us; the launch traced here: 690 us
  blocking collectives  324 us (47%)
  waiting for transfers between devices  253 us (37%)
  local copies, waits for them, and re-layouts  47.8 us (7%)
  matrix products  33 us (5%)
  other arithmetic  16.1 us (2%)
  between operations  15 us (2%)
    psum x1, blocking collectives, local(): lax.psum(row_sums.astype(jnp.bfloat16), 'tensor').astype(jnp.float32)  131 us
    reduce_scatter x1, waiting for transfers between devices, local(): lax.psum_scatter(jnp.dot(hidden, w_down, preferred_element_type=jnp.float...  94.9 us
    pmax x1, blocking collectives, local(): every_max = lax.pmax(jnp.max(logits, axis=1), ('dp', 'tensor'))  86.5 us
    all_gather x1, waiting for transfers between devices, local(): received = lax.all_gather(mid_rows, 'dp', axis=0, tiled=True)  81 us
    all_gather x1, waiting for transfers between devices, local(): key_all = lax.all_gather(key_rows, 'tensor', axis=0, tiled=True)  58.2 us
    all_gather x1, blocking collectives, local(): seg_all = lax.all_gather(segments, 'tensor', axis=0, tiled=True)  46 us
    all_gather x1, blocking collectives, local(): lax.all_gather(last_rows, 'dp', axis=0, tiled=True)  37.8 us
    unnamed x1, blocking collectives  23.2 us
  transfers between devices with their start and end apart: 4, of which 4 were waited for; matrix products, arithmetic and copies ran while one was open for 2% of the time, Pallas kernels for 0%

commit v1 on v0

--- a/solution.py
+++ b/solution.py
@@ -137,7 +137,15 @@
     group_norm = jnp.sqrt(jnp.mean(request_mean * request_mean, axis=1))
     slot_count = lax.axis_size("dp") * REQS
     every_last, every_norm = (
-        lax.all_gather(last_rows, "dp", axis=0, tiled=True),
+        jnp.concatenate(
+            jax.lax.all_to_all(
+                jnp.stack([last_rows] * jax.lax.axis_size("dp")),
+                axis_name="dp",
+                split_axis=0,
+                concat_axis=0,
+            ),
+            axis=0,
+        ),
         lax.all_gather(group_norm, "dp", axis=0, tiled=True),
     )
     logits = jnp.dot(

time: 691 us -> 657 us (0.951)
  blocking collectives: 324 us -> 285 us
    all_gather x1 -> x0, blocking collectives: 37.8 us -> none  [local(): lax.all_gather(last_rows, 'dp', axis=0, tiled=True)]
  transfers between devices with their start and end apart: 4 -> 5, of which waited for: 4 -> 4; matrix products, arithmetic and copies ran while one was open for 2% -> 2% of each run, Pallas kernels for 0% -> 0%
where the time goes in v1:
time: 657 us; the launch traced here: 656 us
  blocking collectives  285 us (43%)
  waiting for transfers between devices  253 us (39%)
  local copies, waits for them, and re-layouts  48.5 us (7%)
  matrix products  33 us (5%)
  other arithmetic  16.1 us (2%)
  between operations  15 us (2%)
    psum x1, blocking collectives, local(): lax.psum(row_sums.astype(jnp.bfloat16), 'tensor').astype(jnp.float32)  131 us
    reduce_scatter x1, waiting for transfers between devices, local(): lax.psum_scatter(jnp.dot(hidden, w_down, preferred_element_type=jnp.float...  94.9 us
    all_gather x1, waiting for transfers between devices, local(): received = lax.all_gather(mid_rows, 'dp', axis=0, tiled=True)  81 us
    pmax x1, blocking collectives, local(): every_max = lax.pmax(jnp.max(logits, axis=1), ('dp', 'tensor'))  80.7 us
    all_gather x1, waiting for transfers between devices, local(): key_all = lax.all_gather(key_rows, 'tensor', axis=0, tiled=True)  58.2 us
    all_gather x1, blocking collectives, local(): seg_all = lax.all_gather(segments, 'tensor', axis=0, tiled=True)  46 us
    unnamed x1, blocking collectives  28 us
    slice x9, local copies, waits for them, and re-layouts, local(): key_part = key_all[begin:begin + step_size]  22.4 us
  transfers between devices with their start and end apart: 5, of which 4 were waited for; matrix products, arithmetic and copies ran while one was open for 2% of the time, Pallas kernels for 0%

profile of v1, /device:TPU:1, one launch (start us, length us, event | category | flops | bytes accessed | tf_op | source)
XLA Modules:
  0.0 655.7 jit_solution(16564018672586010312)
XLA Ops:
  7.2 1.2 fusion.143
  8.5 3.4 fusion.186
  14.2 46.0 %all-gather = s32[1,4096]{1,0:T(1,128)S(1)} all-gather(s32[1,128]{1,0:T(1,128)S(1)} %copy-done.26), channel_id=2, replica_groups=mesh['dp'=8,'tensor'=32] {'tensor'}, dimensions={1}, use_global_device_ids=true | all-gather | bytes 16896 | tf_op jit(solution)/shard_map/all_gather | solution.py:62
  60.5 1.2 fusion.145
  61.7 19.2 %all-gather.7.cloned.1.call-done = bf16[4096,640]{1,0:T(8,128)(2,1)} async-done(((bf16[128,640]{1,0:T(8,128)(2,1)}), bf16[4096,640]{1,0:T(8,128)(2,1)}) %all-gather.7.cloned.1.call-update) | async-done | bytes 5242896 | tf_op jit(solution)/shard_map/all_gather | solution.py:61
  80.8 4.5 fusion.191
  85.3 2.2 copy.69
  87.5 58.2 %all-gather.5.cloned.1.call-done = bf16[4096,640]{1,0:T(8,128)(2,1)} async-done(((bf16[128,640]{1,0:T(8,128)(2,1)}), bf16[4096,640]{1,0:T(8,128)(2,1)}) %all-gather.5.cloned.1.call-update) | async-done | bytes 5242896 | tf_op jit(solution)/shard_map/all_gather | solution.py:60
  145.7 4.9 fusion.192
  150.6 2.2 copy.58
  152.8 2.2 copy.72
  154.9 2.2 copy.70
  157.1 2.2 copy.68
  159.3 2.2 copy.66
  161.5 2.2 copy.64
  163.7 2.2 copy.62
  165.9 2.2 copy.60
  168.1 2.2 copy.73
  170.3 2.2 copy.71
  172.4 2.2 copy.67
  174.6 2.2 copy.65
  176.8 2.2 copy.63
  179.0 1.1 copy.61
  180.1 1.1 copy.59
  181.2 1.8 select_reduce_fusion.6
  190.2 1.8 fusion.4
  192.0 0.7 fusion.100
  193.1 0.7 fusion.124
  193.9 1.6 fusion.12
  195.5 0.7 fusion.127
  196.6 0.7 fusion.94
  197.3 1.6 fusion
  199.0 0.7 fusion.103
  199.7 1.6 fusion.8
  201.4 0.8 fusion.130
  202.5 0.8 fusion.137
  204.8 1.0 multiply_convert_fusion.2
  206.1 81.0 %all-gather.9.cloned.1.call-done = bf16[1024,1280]{1,0:T(8,128)(2,1)} async-done(((bf16[128,1280]{1,0:T(8,128)(2,1)}), bf16[1024,1280]{1,0:T(8,128)(2,1)}) %all-gather.9.cloned.1.call-update) | async-done | bytes 2621456 | tf_op jit(solution)/shard_map/all_gather | solution.py:106
  287.2 5.9 fusion.194
  293.1 8.4 %convolution_convert_fusion = bf16[1024,1280]{1,0:T(8,128)(2,1)} fusion(bf16[640,1280]{1,0:T(8,128)(2,1)S(1)} %copy-done, f32[1024,640]{1,0:T(8,128)} %fusion.194, bf16[1024,1280]{1,0:T(8,128)(2,1)} %all-gather.9.cloned.1.call-done, bf16[1280,640]{1,0:T(8,128)(2,1)S(1)} %copy-done.27, f32[640]{0:T(1024)S(1)} %copy-done.28, f32[640]{0:T(1024)S(1)} %copy-done.29), kind=kOutput, calls=%fused_computation | convolution fusion | flops 3361996800 | bytes 11146240 | tf_op jit(solution)/shard_map/dot_general | solution.py:111
  304.0 94.9 %reduce-scatter.2.cloned.1.call-done = bf16[128,1280]{1,0:T(8,128)(2,1)} async-done(((bf16[1024,1280]{1,0:T(8,128)(2,1)}), bf16[128,1280]{1,0:T(8,128)(2,1)}) %reduce-scatter.2.cloned.1.call-update) | async-done | bytes 327696 | tf_op jit(solution)/shard_map/reduce_scatter | solution.py:110
  398.9 1.1 fusion.142
  400.1 1.3 multiply_reduce_fusion
  401.4 1.4 multiply_convert_fusion.1
  403.2 130.5 %all-reduce.1 = (bf16[4,1280]{1,0:T(4,128)(2,1)S(1)}, bf16[4]{0:T(256)(128)(2,1)S(1)}, bf16[4,1280]{1,0:T(4,128)(2,1)S(1)}) all-reduce(bf16[4,1280]{1,0:T(4,128)(2,1)S(1)} %convolution_convert_fusion.2, bf16[4]{0:T(256)(128)(2,1)S(1)} %convert_reduce_fusion.1, ...), channel_id=1, replica_groups=mesh['dp'=8,'tensor'=32] {'tensor'}, use_global_device_ids=true, to_apply=%region_24.25 | all-reduce | flops 10244 | bytes 40976 | tf_op jit(solution)/shard_map/psum | solution.py:132
  534.4 4.1 all-to-all-start
  538.7 28.0 %all-reduce = f32[32]{0:T(128)S(1)} all-reduce(f32[32]{0:T(128)S(1)} %sqrt_dynamic-update-slice_fusion), channel_id=1, replica_groups=mesh['dp'=8,'tensor'=32] {'dp'}, use_global_device_ids=true, to_apply=%add | all-reduce | flops 32 | bytes 256
  567.7 80.7 %pmax.7 = f32[32]{0:T(128)S(1)} all-reduce(f32[32]{0:T(128)S(1)} %fusion.133), channel_id=1, replica_groups=mesh['dp'=8,'tensor'=32] {'dp','tensor'}, use_global_device_ids=true, to_apply=%region_33.34 | all-reduce | flops 32 | bytes 256 | tf_op jit(solution)/shard_map/pmax | solution.py:154
  (134 shorter events, 17.2 us)
Async XLA Ops:
  7.2 285.9 %copy-start = (bf16[640,1280]{1,0:T(8,128)(2,1)S(1)}, bf16[640,1280]{1,0:T(8,128)(2,1)}, u32[]{:S(2)}) copy-start(bf16[640,1280]{1,0:T(8,128)(2,1)} %param.26) | copy-start | bytes 4915204
  7.2 73.7 %all-gather.7.cloned.1.call-start = ((), (), s32[]{:S(2)}) async-start(), calls=%async_computation.3 | async-start | bytes 5406720 | tf_op jit(solution)/shard_map/all_gather | solution.py:61
  11.9 1.2 copy-start.25
  12.6 1.6 copy-start.26
  12.6 133.1 %all-gather.5.cloned.1.call-start = ((), (), s32[]{:S(2)}) async-start(), calls=%async_computation.2 | async-start | bytes 5406720 | tf_op jit(solution)/shard_map/all_gather | solution.py:60
  13.9 273.3 %all-gather.9.cloned.1.call-start = ((), (), s32[]{:S(2)}) async-start(), calls=%async_computation.4 | async-start | bytes 2949120 | tf_op jit(solution)/shard_map/all_gather | solution.py:106
  180.1 2.9 copy-start.10
  181.2 1.8 copy-start.21
  183.0 1.1 copy-start.9
  183.0 1.1 copy-start.20
  183.7 1.1 copy-start.8
  184.7 1.1 copy-start.7
  185.5 1.1 copy-start.6
  186.5 1.1 copy-start.5
  187.3 1.1 copy-start.4
  188.3 1.1 copy-start.19
  190.2 1.8 copy-start.18
  192.0 1.1 copy-start.17
  193.8 1.6 copy-start.15
  195.5 1.1 copy-start.16
  197.3 1.6 copy-start.14
  199.7 1.7 copy-start.13
  201.4 1.1 copy-start.12
  202.5 1.4 copy-start.11
  202.5 2.0 copy-start.23
  203.3 1.2 copy-start.1
  205.8 87.3 %copy-start.27 = (bf16[1280,640]{1,0:T(8,128)(2,1)S(1)}, bf16[1280,640]{1,0:T(8,128)(2,1)}, u32[]{:S(2)}) copy-start(bf16[1280,640]{1,0:T(8,128)(2,1)} %param.23) | copy-start | bytes 4915204
  205.8 87.2 %copy-start.28 = (f32[640]{0:T(1024)S(1)}, f32[640]{0:T(1024)}, u32[]{:S(2)}) copy-start(f32[640]{0:T(1024)} %param.25) | copy-start | bytes 7684
  205.8 87.2 %copy-start.29 = (f32[640]{0:T(1024)S(1)}, f32[640]{0:T(1024)}, u32[]{:S(2)}) copy-start(f32[640]{0:T(1024)} %param.24) | copy-start | bytes 7684
  205.9 193.1 %reduce-scatter.2.cloned.1.call-start = ((), (), s32[]{:S(2)}) async-start(), calls=%async_computation.5 | async-start | bytes 2949120 | tf_op jit(solution)/shard_map/reduce_scatter | solution.py:110
  301.5 0.7 copy-start.30
  301.5 0.7 copy-start.32
  301.5 98.5 %copy-start.2 = (bf16[128,1280]{1,0:T(8,128)(2,1)S(1)}, bf16[128,1280]{1,0:T(8,128)(2,1)}, u32[]{:S(2)}) copy-start(bf16[128,1280]{1,0:T(8,128)(2,1)} %multiply_convert_fusion.2) | copy-start | bytes 983044
  301.5 98.5 %copy-start.24 = (f32[1280]{0:T(1024)S(1)}, f32[1280]{0:T(1024)}, u32[]{:S(2)}) copy-start(f32[1280]{0:T(1024)} %param.27) | copy-start | bytes 15364
  301.5 265.2 %copy-start.22 = (bf16[1280,125]{1,0:T(8,128)(2,1)S(1)}, bf16[1280,125]{1,0:T(8,128)(2,1)}, u32[]{:S(2)}) copy-start(bf16[1280,125]{1,0:T(8,128)(2,1)} %param.28) | copy-start | bytes 960004
  301.5 265.5 %copy-start.31 = (s32[32]{0:T(128)S(1)}, s32[32]{0:T(128)}, u32[]{:S(2)}) copy-start(s32[32]{0:T(128)} %param.17) | copy-start | bytes 388
  402.8 246.4 %copy-start.3 = (bf16[128,1280]{1,0:T(8,128)(2,1)}, bf16[128,1280]{1,0:T(8,128)(2,1)S(1)}, u32[]{:S(2)}) copy-start(bf16[128,1280]{1,0:T(8,128)(2,1)S(1)} %multiply_convert_fusion.1) | copy-start | bytes 983044
  534.4 32.3 %all-to-all-start = ((bf16[8,4,1280]{2,1,0:T(4,128)(2,1)}), bf16[8,4,1280]{2,1,0:T(4,128)(2,1)S(1)}, u32[]{:S(2)}, u32[]{:S(2)}) async-start(bf16[8,4,1280]{2,1,0:T(4,128)(2,1)} %stack.2), calls=%async_computation.1 | async-start | bytes 163840 | tf_op jit(solution)/shard_map/all_to_all | solution.py:141
Sparse Core Ops, SparseCore 0:
  12.7 68.0 all-gather.6
  82.7 62.9 all-gather.4
  205.9 81.1 all-gather.8
  301.7 97.1 reduce-scatter.1
